TPU v7x, 32 devices: a whole 2x2x4 slice. The times are simulated.
32 devices in a mesh: tm: 4 (over y, x), height: 2 (over core), chan: 4 (over z).
Axes of the slice: x: 2, y: 2, z: 4, core: 2. Of those that a mesh axis runs over, the one named last changes fastest.
Arguments:
- features: bfloat16 [384, 8, 8, 160], P('chan', 'tm', 'height'), may hold values from -400 to 400, as said below
- cotangent: bfloat16 [384, 8, 8, 160], P('chan', 'tm', 'height'), may hold values from -6 to 6
- conv_weight: bfloat16 [384, 27, 384], P('chan'), may hold values from -0.0625 to 0.0625
- norm_gain: float32 [384], replicated, may hold values from 0.5 to 1.5
- norm_bias: float32 [384], replicated, may hold values from -3 to 3
Outputs:
- input_grad: bfloat16 [384, 8, 8, 160], P('chan', 'tm', 'height')
- weight_grad: float32 [384, 27, 384], P('chan')
Inputs may be any that keep to these rules, and one draw needn't show every extreme that they name: `features`: bounded activations.
All inputs are finite; a program needn't handle non-finite values.
Results may differ from a plain program's by a relative error of at most 0.003.
Values may be sent and summed in bfloat16 or wider, within the bound.
No kernel may reach another device: no remote copies, remote signals or barrier semaphores. Data moves between devices by JAX's collectives and lax.ppermute only.
A program may use at most 64 MiB of HBM per device.

v0:
```python
import math
import jax
import jax.numpy as jnp
from jax import lax
from jax.sharding import PartitionSpec as P


def from_behind(block, axis, distance):
    devices = range(lax.axis_size(axis))
    route = [(i - distance, i) for i in devices if i - distance in devices]
    return lax.ppermute(block, axis, route)


def with_halo(array, sides, width):
    for axis, dim in sides:
        size, length = (lax.axis_size(axis), array.shape[dim])
        up = [(i, (i + 1) % size) for i in range(size - 1)]
        down = [(j, i) for i, j in up]
        last = lax.slice_in_dim(array, length - width, length, axis=dim)
        first = lax.slice_in_dim(array, 0, width, axis=dim)
        before = lax.ppermute(last, axis, up)
        after = lax.ppermute(first, axis, down)
        array = jnp.concatenate([before, array, after], axis=dim)
    return array


def on_device(features, cotangent, conv_weight, norm_gain, norm_bias):
    chans, frames, rows, cols = features.shape
    whole_x = lax.all_gather(features, "chan", axis=0, tiled=True)
    total = whole_x.shape[0]
    flat_x = whole_x.reshape(total, -1).astype(jnp.float32)
    inv_rms = lax.rsqrt(jnp.mean(flat_x * flat_x, axis=0, keepdims=True) + 1e-06)
    normed = flat_x * inv_rms * norm_gain[:, None] + norm_bias[:, None]
    active = jax.nn.silu(normed).astype(jnp.bfloat16)
    ahead = from_behind(cotangent, "tm", -1)
    longer = jnp.concatenate([cotangent, ahead], axis=1)
    bordered = with_halo(longer, (("height", 2),), 1)
    padded = jnp.pad(bordered, ((0, 0), (0, 0), (0, 0), (1, 1)))
    taps = []
    for kt in range(3):
        for kh in range(3):
            for kw in range(3):
                taps.append(
                    padded[
                        :, 2 - kt : 2 - kt + frames, 2 - kh : 2 - kh + rows, 2 - kw : 2 - kw + cols
                    ]
                )
    stacked = jnp.stack(taps, axis=1).reshape(chans * 27, -1)
    local_sums = lax.dot_general(
        stacked, active, (((1,), (1,)), ((), ())), preferred_element_type=jnp.float32
    )
    positions = frames * lax.axis_size("tm") * rows * lax.axis_size("height") * cols
    summed = lax.psum(local_sums, ("tm", "height"))
    weight_grad = (summed / math.sqrt(positions)).reshape(chans, 27, total)
    sig = jax.nn.sigmoid(normed)
    slope = sig * (1.0 + normed * (1.0 - sig))
    offset = lax.axis_index("chan") * chans
    weight_part = conv_weight.reshape(chans * 27, chans * lax.axis_size("chan"))
    act_grad = lax.psum_scatter(
        lax.dot_general(
            weight_part, stacked, (((0,), (0,)), ((), ())), preferred_element_type=jnp.float32
        ),
        "chan",
        scatter_dimension=0,
        tiled=True,
    )
    own_x = features.reshape(chans, -1).astype(jnp.float32)
    own_slope = lax.dynamic_slice_in_dim(slope, offset, chans, 0)
    own_gain = lax.dynamic_slice_in_dim(norm_gain, offset, chans, 0)
    upstream = act_grad * own_slope * own_gain[:, None]
    dots = lax.psum(jnp.sum(upstream * own_x, axis=0, keepdims=True), "chan")
    own_back = inv_rms * upstream - own_x * inv_rms**3 * dots / total
    result = cotangent.reshape(chans, -1).astype(jnp.float32) + own_back
    return (result.astype(jnp.bfloat16).reshape(features.shape), weight_grad)


def solution(mesh):
    return jax.shard_map(
        on_device,
        mesh=mesh,
        in_specs=(
            P("chan", "tm", "height", None),
            P("chan", "tm", "height", None),
            P("chan", None, None),
            P(),
            P(),
        ),
        out_specs=(P("chan", "tm", "height", None), P("chan", None, None)),
        check_vma=False,
    )
```

profile of v0, /device:TPU:0, one launch (start us, length us, event | category | flops | bytes accessed | tf_op | source)
XLA Modules:
  0.0 245.2 jit_solution(13448478375143645336)
XLA Ops:
  8.0 1.3 collective-permute-start
  9.3 1.3 copy.16
  10.7 31.4 %all_gather.3 = bf16[384,2,4,160]{3,2,1,0:T(4,128)(2,1)S(1)} all-gather(bf16[96,2,4,160]{3,2,1,0:T(4,128)(2,1)S(1)} %copy.16), channel_id=1, replica_groups=mesh['tm'=4,'height'=2,'chan'=4] {'chan'}, dimensions={0}, use_global_device_ids=true | all-gather | bytes 1228800 | tf_op jit(solution)/shard_map/all_gather | solution.py:29
  42.1 1.4 copy.17
  43.9 1.0 constant_dynamic-update-slice_fusion.1
  45.0 1.3 collective-permute-start.1
  46.3 1.3 collective-permute-start.2
  47.6 1.4 multiply_convert_fusion
  71.3 21.1 %copy.18 = bf16[96,27,2,4,160]{4,3,2,1,0:T(4,128)(2,1)} copy(bf16[96,27,2,4,160]{0,4,3,2,1:T(8,128)(2,1)} %fusion.31) | data formatting | bytes 13271040 | tf_op jit(solution)/shard_map/stack | solution.py:48
  92.5 20.4 %reshape.67 = bf16[2592,1280]{1,0:T(8,128)(2,1)} reshape(bf16[96,27,2,4,160]{4,3,2,1,0:T(4,128)(2,1)} %copy.18) | data formatting | bytes 13271040 | tf_op jit(solution)/shard_map/reshape | solution.py:48
  112.8 8.4 %fusion.56 = f32[2592,384]{1,0:T(8,128)} fusion(bf16[2592,1280]{1,0:T(8,128)(2,1)} %reshape.67, bf16[384,1280]{0,1:T(8,128)(2,1)S(1)} %bitcast.128), kind=kOutput, calls=%fused_computation.102 | convolution fusion | flops 2548039680 | bytes 11599872 | tf_op jit(solution)/shard_map/dot_general | solution.py:49
  121.5 2.3 copy.19
  123.8 2.2 reshape.68
  126.0 6.7 %convolution_bitcast_fusion = f32[384,1280]{0,1:T(8,128)S(1)} fusion(bf16[2592,1280]{1,0:T(8,128)(2,1)} %reshape.67, bf16[2592,384]{1,0:T(8,128)(2,1)} %reshape.68), kind=kOutput, calls=%fused_computation.2 | convolution fusion | flops 2548039680 | bytes 10592256 | tf_op jit(solution)/shard_map/dot_general | solution.py:60
  132.7 1.8 copy.21
  134.7 1.8 negate_exponential_fusion
  136.5 66.4 %all-reduce.3.cloned.1.call-done = f32[2592,384]{1,0:T(8,128)} async-done(((f32[2592,384]{1,0:T(8,128)}), f32[2592,384]{1,0:T(8,128)}) %all-reduce.3.cloned.1.call-update) | async-done | bytes 3981328 | tf_op jit(solution)/shard_map/psum | solution.py:53
  202.9 4.4 %broadcast_multiply_fusion = f32[2592,384]{1,0:T(8,128)} fusion(f32[2592,384]{1,0:T(8,128)} %all-reduce.3.cloned.1.call-done), kind=kLoop, calls=%fused_computation.4 | loop fusion | flops 995328 | bytes 7962624 | tf_op jit(solution)/shard_map/div | solution.py:54
  207.3 5.0 %reshape.70 = f32[96,27,384]{2,1,0:T(8,128)} reshape(f32[2592,384]{1,0:T(8,128)} %broadcast_multiply_fusion) | data formatting | bytes 7962624 | tf_op jit(solution)/shard_map/reshape | solution.py:54
  212.3 6.6 %copy.20 = f32[96,27,384]{2,0,1:T(8,128)} copy(f32[96,27,384]{2,1,0:T(8,128)} %reshape.70) | data formatting | bytes 7962624
  218.8 2.1 copy.22
  221.0 2.8 %fusion.13 = (f32[1280]{0:T(1024)S(1)}, f32[96,1280]{0,1:T(8,128)}) fusion(bf16[96,2,4,160]{0,3,2,1:T(8,128)(2,1)S(1)} %copy-done.2, f32[96]{0:T(128)S(1)} %dynamic_slice.7, f32[96,1280]{0,1:T(8,128)} %copy.22, f32[384,1280]{0,1:T(8,128)} %get-tuple-element.13, s32[]{:T(128)S(6)} %select_n.4, f32[384,1280]{0,1:T(8,128)S(1)} %get-tuple-element.12), kind=kLoop, calls=%fused_computation.31 | loop fusion | flops 1350400 | bytes 2217348 | tf_op jit(solution)/shard_map/reduce_sum | solution.py:71
  223.8 11.6 %psum.14 = f32[1280]{0:T(1024)S(1)} all-reduce(f32[1280]{0:T(1024)S(1)} %get-tuple-element.10), channel_id=1, replica_groups=mesh['tm'=4,'height'=2,'chan'=4] {'chan'}, use_global_device_ids=true, to_apply=%region_3.4 | all-reduce | flops 1280 | bytes 10240 | tf_op jit(solution)/shard_map/psum | solution.py:71
  235.4 2.4 fusion.12
  (53 shorter events, 23.2 us)
Async XLA Ops:
  8.0 194.9 %all-reduce.3.cloned.1.call-start = ((), (), s32[]{:S(2)}) async-start(), calls=%async_computation.1 | async-start | bytes 7962624 | tf_op jit(solution)/shard_map/psum | solution.py:53
  8.0 36.9 %collective-permute-start = (bf16[96,2,4,160]{0,3,2,1:T(8,128)(2,1)}, bf16[96,2,4,160]{0,3,2,1:T(8,128)(2,1)S(1)}, u32[]{:S(2)}, u32[]{:S(2)}) collective-permute-start(bf16[96,2,4,160]{0,3,2,1:T(8,128)(2,1)} %param.6), channel_id=1, source_target_pairs={{8,0},{16,8},{24,16},{9,1},{17,9},{25,17},{10,2},{18,10},{26,18},{... | collective-permute-start | bytes 737288 | tf_op jit(solution)/shard_map/ppermute | solution.py:11
  45.0 4.0 %collective-permute-start.1 = (bf16[96,4,1,160]{0,3,2,1:T(8,128)(2,1)S(1)}, bf16[96,4,1,160]{0,3,2,1:T(8,128)(2,1)S(1)}, u32[]{:S(2)}, u32[]{:S(2)}) collective-permute-start(bf16[96,4,1,160]{0,3,2,1:T(8,128)(2,1)S(1)} %get-tuple-element.14), channel_id=1, source_target_pairs={{0,4},{1,5},{2,6},{3,7},{8,12},{9,13},{10,14},{11,15},{16,20},{17,... | collective-permute-start | bytes 368648 | tf_op jit(solution)/shard_map/ppermute | solution.py:21
  46.3 3.3 %collective-permute-start.2 = (bf16[96,4,1,160]{0,3,2,1:T(8,128)(2,1)S(1)}, bf16[96,4,1,160]{0,3,2,1:T(8,128)(2,1)S(1)}, u32[]{:S(2)}, u32[]{:S(2)}) collective-permute-start(bf16[96,4,1,160]{0,3,2,1:T(8,128)(2,1)S(1)} %get-tuple-element.15), channel_id=1, source_target_pairs={{4,0},{5,1},{6,2},{7,3},{12,8},{13,9},{14,10},{15,11},{20,16},{21,... | collective-permute-start | bytes 368648 | tf_op jit(solution)/shard_map/ppermute | solution.py:22
  50.0 17.4 %copy-start = (bf16[96,2,4,160]{0,3,2,1:T(8,128)(2,1)S(1)}, bf16[96,2,4,160]{0,3,2,1:T(8,128)(2,1)}, u32[]{:S(2)}) copy-start(bf16[96,2,4,160]{0,3,2,1:T(8,128)(2,1)} %param.6) | copy-start | bytes 737284
  121.3 97.5 %reduce-scatter.4.cloned.1.call-start = ((), (), s32[]{:S(2)}) async-start(), calls=%async_computation.2 | async-start | bytes 2457600
  126.0 8.6 %copy-start.3 = (f32[384]{0:T(512)S(1)}, f32[384]{0:T(512)}, u32[]{:S(2)}) copy-start(f32[384]{0:T(512)} %param.8) | copy-start | bytes 4612
  126.0 8.7 %copy-start.4 = (f32[384]{0:T(512)S(1)}, f32[384]{0:T(512)}, u32[]{:S(2)}) copy-start(f32[384]{0:T(512)} %param.9) | copy-start | bytes 4612
  207.3 13.7 %copy-start.2 = (bf16[96,2,4,160]{0,3,2,1:T(8,128)(2,1)S(1)}, bf16[96,2,4,160]{0,3,2,1:T(8,128)(2,1)}, u32[]{:S(2)}) copy-start(bf16[96,2,4,160]{0,3,2,1:T(8,128)(2,1)} %param.5) | copy-start | bytes 737284
  207.3 28.1 %copy-start.1 = (bf16[96,2,4,160]{0,3,2,1:T(8,128)(2,1)S(1)}, bf16[96,2,4,160]{0,3,2,1:T(8,128)(2,1)}, u32[]{:S(2)}) copy-start(bf16[96,2,4,160]{0,3,2,1:T(8,128)(2,1)} %param.6) | copy-start | bytes 737284
Sparse Core Ops, SparseCore 0:
  121.4 81.3 all-reduce.2
Sparse Core Ops, SparseCore 1:
  134.6 44.6 reduce-scatter.3
where the time goes:
time: 247 us; the launch traced here: 245 us
  local copies, waits for them, and re-layouts  82 us (33%)
  waiting for transfers between devices  67 us (27%)
  blocking collectives  43 us (17%)
  other arithmetic  18.3 us (7%)
  between operations  15.6 us (6%)
  matrix products  15.1 us (6%)
  starting transfers between devices  4.15 us (2%)
    psum x1, waiting for transfers between devices, on_device(): summed = lax.psum(local_sums, ('tm', 'height'))  66.4 us
    all_gather x1, blocking collectives, on_device(): whole_x = lax.all_gather(features, 'chan', axis=0, tiled=True)  31.4 us
    unnamed x36, local copies, waits for them, and re-layouts  30.9 us
    another operation x2, local copies, waits for them, and re-layouts, on_device(): stacked = jnp.stack(taps, axis=1).reshape(chans * 27, -1)  21.9 us
    reshape x1, local copies, waits for them, and re-layouts, on_device(): stacked = jnp.stack(taps, axis=1).reshape(chans * 27, -1)  20.4 us
    psum x1, blocking collectives, on_device(): dots = lax.psum(jnp.sum(upstream * own_x, axis=0, keepdims=True), 'chan')  11.6 us
    dot_general x1, matrix products, on_device(): lax.dot_general(stacked, active, (((1,), (1,)), ((), ())), preferred_elem...  8.42 us
    dot_general x1, matrix products, on_device(): lax.dot_general(weight_part, stacked, (((0,), (0,)), ((), ())), preferred...  6.67 us
  transfers between devices with their start and end apart: 5, of which 2 were waited for; matrix products, arithmetic and copies ran while one was open for 15% of the time, Pallas kernels for 0%

commit v1 on v0

--- a/solution.py
+++ b/solution.py
@@ -3,6 +3,7 @@
 import jax.numpy as jnp
 from jax import lax
 from jax.sharding import PartitionSpec as P
+from jax.lax import psum
 
 
 def from_behind(block, axis, distance):
@@ -50,7 +51,7 @@
         stacked, active, (((1,), (1,)), ((), ())), preferred_element_type=jnp.float32
     )
     positions = frames * lax.axis_size("tm") * rows * lax.axis_size("height") * cols
-    summed = lax.psum(local_sums, ("tm", "height"))
+    summed = psum(psum(local_sums, axis_name="height"), "tm")
     weight_grad = (summed / math.sqrt(positions)).reshape(chans, 27, total)
     sig = jax.nn.sigmoid(normed)
     slope = sig * (1.0 + normed * (1.0 - sig))

time: 247 us -> 282 us (1.14)
  waiting for transfers between devices: 67 us -> 104 us
    unnamed x3 -> x4, waiting for transfers between devices: 0.03 us -> 25.3 us
    psum x1 -> x2, waiting for transfers between devices: 66.4 us -> 78.6 us  [on_device(): summed = psum(psum(local_sums, axis_name='height'), 'tm')]
    unnamed x36 -> x34, local copies, waits for them, and re-layouts: 30.9 us -> 30.9 us
  transfers between devices with their start and end apart: 5 -> 6, of which waited for: 2 -> 4; matrix products, arithmetic and copies ran while one was open for 15% -> 10% of each run, Pallas kernels for 0% -> 0%
where the time goes in v1:
time: 282 us; the launch traced here: 280 us
  waiting for transfers between devices  104 us (37%)
  local copies, waits for them, and re-layouts  82 us (29%)
  blocking collectives  41.4 us (15%)
  other arithmetic  17.6 us (6%)
  between operations  15.7 us (6%)
  matrix products  15.1 us (5%)
  starting transfers between devices  4.19 us (1%)
    psum x2, waiting for transfers between devices, on_device(): summed = psum(psum(local_sums, axis_name='height'), 'tm')  78.6 us
    all_gather x1, blocking collectives, on_device(): whole_x = lax.all_gather(features, 'chan', axis=0, tiled=True)  31.4 us
    unnamed x34, local copies, waits for them, and re-layouts  30.9 us
    unnamed x4, waiting for transfers between devices  25.3 us
    another operation x2, local copies, waits for them, and re-layouts, on_device(): stacked = jnp.stack(taps, axis=1).reshape(chans * 27, -1)  21.9 us
    reshape x1, local copies, waits for them, and re-layouts, on_device(): stacked = jnp.stack(taps, axis=1).reshape(chans * 27, -1)  20.4 us
    psum x1, blocking collectives, on_device(): dots = lax.psum(jnp.sum(upstream * own_x, axis=0, keepdims=True), 'chan')  9.94 us
    dot_general x1, matrix products, on_device(): lax.dot_general(stacked, active, (((1,), (1,)), ((), ())), preferred_elem...  8.42 us
  transfers between devices with their start and end apart: 6, of which 4 were waited for; matrix products, arithmetic and copies ran while one was open for 10% of the time, Pallas kernels for 0%

profile of v1, /device:TPU:0, one launch (start us, length us, event | category | flops | bytes accessed | tf_op | source)
XLA Modules:
  0.0 280.4 jit_solution(10245791537675759909)
XLA Ops:
  8.0 1.3 collective-permute-start
  9.3 1.3 copy.16
  10.7 31.4 %all_gather.3 = bf16[384,2,4,160]{3,2,1,0:T(4,128)(2,1)S(1)} all-gather(bf16[96,2,4,160]{3,2,1,0:T(4,128)(2,1)S(1)} %copy.16), channel_id=1, replica_groups=mesh['tm'=4,'height'=2,'chan'=4] {'chan'}, dimensions={0}, use_global_device_ids=true | all-gather | bytes 1228800 | tf_op jit(solution)/shard_map/all_gather | solution.py:30
  42.1 1.4 copy.17
  45.0 1.3 collective-permute-start.1
  47.6 1.4 multiply_convert_fusion
  71.2 21.2 %copy.18 = bf16[96,27,2,4,160]{4,3,2,1,0:T(4,128)(2,1)} copy(bf16[96,27,2,4,160]{0,4,3,2,1:T(8,128)(2,1)} %fusion.31) | data formatting | bytes 13271040 | tf_op jit(solution)/shard_map/stack | solution.py:49
  92.4 20.4 %reshape.67 = bf16[2592,1280]{1,0:T(8,128)(2,1)} reshape(bf16[96,27,2,4,160]{4,3,2,1,0:T(4,128)(2,1)} %copy.18) | data formatting | bytes 13271040 | tf_op jit(solution)/shard_map/reshape | solution.py:49
  112.8 8.4 %fusion.56 = f32[2592,384]{1,0:T(8,128)} fusion(bf16[2592,1280]{1,0:T(8,128)(2,1)} %reshape.67, bf16[384,1280]{0,1:T(8,128)(2,1)S(1)} %bitcast.128), kind=kOutput, calls=%fused_computation.102 | convolution fusion | flops 2548039680 | bytes 11599872 | tf_op jit(solution)/shard_map/dot_general | solution.py:50
  121.5 2.3 copy.19
  123.8 2.2 reshape.68
  126.0 6.6 %convolution_bitcast_fusion = f32[384,1280]{0,1:T(8,128)S(1)} fusion(bf16[2592,1280]{1,0:T(8,128)(2,1)} %reshape.67, bf16[2592,384]{1,0:T(8,128)(2,1)} %reshape.68), kind=kOutput, calls=%fused_computation.2 | convolution fusion | flops 2548039680 | bytes 10592256 | tf_op jit(solution)/shard_map/dot_general | solution.py:61
  132.7 1.9 copy.21
  134.6 17.5 %all-reduce.4.cloned.1.call-done = f32[2592,384]{1,0:T(8,128)} async-done(((f32[2592,384]{1,0:T(8,128)}), f32[2592,384]{1,0:T(8,128)}) %all-reduce.4.cloned.1.call-update) | async-done | bytes 3981328 | tf_op jit(solution)/shard_map/psum | solution.py:54
  152.3 1.7 negate_exponential_fusion
  154.0 25.2 %reduce-scatter.4.cloned.1.call-done = f32[96,1280]{1,0:T(8,128)} async-done(((f32[384,1280]{1,0:T(8,128)}), f32[96,1280]{1,0:T(8,128)}) %reduce-scatter.4.cloned.1.call-update) | async-done | bytes 491536
  179.2 2.2 copy.22
  181.4 2.3 fusion.13
  183.6 9.9 %psum.21 = f32[1280]{0:T(1024)S(1)} all-reduce(f32[1280]{0:T(1024)S(1)} %get-tuple-element.10), channel_id=1, replica_groups=mesh['tm'=4,'height'=2,'chan'=4] {'chan'}, use_global_device_ids=true, to_apply=%region_3.4 | all-reduce | flops 1280 | bytes 10240 | tf_op jit(solution)/shard_map/psum | solution.py:72
  193.6 2.3 fusion.12
  195.9 61.1 %all-reduce.6.cloned.1.call-done = f32[2592,384]{1,0:T(8,128)} async-done(((f32[2592,384]{1,0:T(8,128)}), f32[2592,384]{1,0:T(8,128)}) %all-reduce.6.cloned.1.call-update) | async-done | bytes 3981328 | tf_op jit(solution)/shard_map/psum | solution.py:54
  257.0 4.4 %broadcast_multiply_fusion = f32[2592,384]{1,0:T(8,128)} fusion(f32[2592,384]{1,0:T(8,128)} %all-reduce.6.cloned.1.call-done), kind=kLoop, calls=%fused_computation.4 | loop fusion | flops 995328 | bytes 7962624 | tf_op jit(solution)/shard_map/div | solution.py:55
  261.4 4.9 %reshape.70 = f32[96,27,384]{2,1,0:T(8,128)} reshape(f32[2592,384]{1,0:T(8,128)} %broadcast_multiply_fusion) | data formatting | bytes 7962624 | tf_op jit(solution)/shard_map/reshape | solution.py:55
  266.4 6.6 %copy.20 = f32[96,27,384]{2,0,1:T(8,128)} copy(f32[96,27,384]{2,1,0:T(8,128)} %reshape.70) | data formatting | bytes 7962624
  (54 shorter events, 25.4 us)
Async XLA Ops:
  8.0 144.1 %all-reduce.4.cloned.1.call-start = ((), (), s32[]{:S(2)}) async-start(), calls=%async_computation.1 | async-start | bytes 7962624 | tf_op jit(solution)/shard_map/psum | solution.py:54
  8.0 36.9 %collective-permute-start = (bf16[96,2,4,160]{0,3,2,1:T(8,128)(2,1)}, bf16[96,2,4,160]{0,3,2,1:T(8,128)(2,1)S(1)}, u32[]{:S(2)}, u32[]{:S(2)}) collective-permute-start(bf16[96,2,4,160]{0,3,2,1:T(8,128)(2,1)} %param.6), channel_id=1, source_target_pairs={{8,0},{16,8},{24,16},{9,1},{17,9},{25,17},{10,2},{18,10},{26,18},{... | collective-permute-start | bytes 737288 | tf_op jit(solution)/shard_map/ppermute | solution.py:12
  45.0 4.0 %collective-permute-start.1 = (bf16[96,4,1,160]{0,3,2,1:T(8,128)(2,1)S(1)}, bf16[96,4,1,160]{0,3,2,1:T(8,128)(2,1)S(1)}, u32[]{:S(2)}, u32[]{:S(2)}) collective-permute-start(bf16[96,4,1,160]{0,3,2,1:T(8,128)(2,1)S(1)} %get-tuple-element.14), channel_id=1, source_target_pairs={{0,4},{1,5},{2,6},{3,7},{8,12},{9,13},{10,14},{11,15},{16,20},{17,... | collective-permute-start | bytes 368648 | tf_op jit(solution)/shard_map/ppermute | solution.py:22
  46.3 3.3 %collective-permute-start.2 = (bf16[96,4,1,160]{0,3,2,1:T(8,128)(2,1)S(1)}, bf16[96,4,1,160]{0,3,2,1:T(8,128)(2,1)S(1)}, u32[]{:S(2)}, u32[]{:S(2)}) collective-permute-start(bf16[96,4,1,160]{0,3,2,1:T(8,128)(2,1)S(1)} %get-tuple-element.15), channel_id=1, source_target_pairs={{4,0},{5,1},{6,2},{7,3},{12,8},{13,9},{14,10},{15,11},{20,16},{21,... | collective-permute-start | bytes 368648 | tf_op jit(solution)/shard_map/ppermute | solution.py:23
  50.0 17.4 %copy-start = (bf16[96,2,4,160]{0,3,2,1:T(8,128)(2,1)S(1)}, bf16[96,2,4,160]{0,3,2,1:T(8,128)(2,1)}, u32[]{:S(2)}) copy-start(bf16[96,2,4,160]{0,3,2,1:T(8,128)(2,1)} %param.6) | copy-start | bytes 737284
  121.3 58.0 %reduce-scatter.4.cloned.1.call-start = ((), (), s32[]{:S(2)}) async-start(), calls=%async_computation.3 | async-start | bytes 2457600
  132.6 19.6 %copy-start.2 = (f32[384]{0:T(512)S(1)}, f32[384]{0:T(512)}, u32[]{:S(2)}) copy-start(f32[384]{0:T(512)} %param.8) | copy-start | bytes 4612
  132.6 19.6 %copy-start.3 = (f32[384]{0:T(512)S(1)}, f32[384]{0:T(512)}, u32[]{:S(2)}) copy-start(f32[384]{0:T(512)} %param.9) | copy-start | bytes 4612
  132.7 60.9 %copy-start.1 = (bf16[96,2,4,160]{0,3,2,1:T(8,128)(2,1)S(1)}, bf16[96,2,4,160]{0,3,2,1:T(8,128)(2,1)}, u32[]{:S(2)}) copy-start(bf16[96,2,4,160]{0,3,2,1:T(8,128)(2,1)} %param.6) | copy-start | bytes 737284
  134.6 122.5 %all-reduce.6.cloned.1.call-start = ((), (), s32[]{:S(2)}) async-start(), calls=%async_computation.2 | async-start | bytes 7962624 | tf_op jit(solution)/shard_map/psum | solution.py:54
Sparse Core Ops, SparseCore 0:
  121.4 30.6 all-reduce.3
  155.5 101.5 all-reduce.5
Sparse Core Ops, SparseCore 1:
  134.6 44.5 reduce-scatter.3
